TPU v7x, 512 devices: a whole 4x8x8 slice. The times are simulated.
512 devices in a mesh: row: 16 (over y, z_hi), col: 32 (over x, z_lo, core).
Axes of the slice: x: 4, y: 8, z: 8 (z_hi: 2, z_lo: 4; z = z_hi * 4 + z_lo), core: 2. Of those that a mesh axis runs over, the one named last changes fastest.
Arguments:
- points: bfloat16 [81920, 128], P(('row', 'col')), may hold values from -6 to 6
- w_in: bfloat16 [128, 1024], replicated, may hold values from -0.5 to 0.5
- w_mid: bfloat16 [1024, 1024], replicated, may hold values from -0.1875 to 0.1875
- w_out: bfloat16 [1024, 32], replicated, may hold values from -0.1875 to 0.1875
- lengthscale: float32 [32], replicated, may hold values from 1 to 10
- probes: bfloat16 [8, 81920], P(None, ('row', 'col')), may hold values from -0.0546875 to 0.0546875
Outputs:
- kv: float32 [8, 81920], P(None, ('row', 'col'))
All inputs are finite; a program needn't handle non-finite values.
Results may differ from a plain program's by a relative error of at most 0.0055.
Values may be sent and summed in bfloat16 or wider, within the bound.
No kernel may reach another device: no remote copies, remote signals or barrier semaphores. Data moves between devices by JAX's collectives and lax.ppermute only.
A program may use at most 64 MiB of HBM per device.

v0:
```python
import jax
import jax.numpy as jnp
from jax import lax
from jax.sharding import PartitionSpec as P


def wide_general(left, right, dims):
    return lax.dot_general(
        left.astype(jnp.float32),
        right.astype(jnp.float32),
        (dims, ((), ())),
        precision=lax.Precision.HIGHEST,
    )


def matern_tile(left_feats, left_sq, right_feats):
    cross_term = wide_general(left_feats, right_feats, ((0,), (0,)))
    right_wide = right_feats.astype(jnp.float32)
    right_sq = jnp.sum(right_wide * right_wide, axis=0)
    dist_sq = jnp.maximum(left_sq[:, None] + right_sq[None, :] - 2.0 * cross_term, 0.0)
    scaled_dist = jnp.sqrt(5.0 * dist_sq)
    values = (1.0 + scaled_dist + scaled_dist * scaled_dist / 3.0) * jnp.exp(-scaled_dist)
    return values.astype(jnp.bfloat16)


def block_width(columns):
    for candidate in (256, 384, 128):
        return candidate
    return columns


def on_device(points, w_in, w_mid, w_out, lengthscale, probes):
    hidden_one = jax.nn.relu(wide_general(points, w_in, ((1,), (0,)))).astype(jnp.bfloat16)
    hidden_two = jax.nn.relu(wide_general(hidden_one, w_mid, ((1,), (0,)))).astype(jnp.bfloat16)
    features = wide_general(w_out, hidden_two, ((0,), (1,)))
    scaled = (features / lengthscale[:, None]).astype(jnp.bfloat16)
    probe_rows = probes.shape[0]
    row_feats = lax.all_gather(scaled, "col", axis=1, tiled=True)
    row_wide = row_feats.astype(jnp.float32)
    row_sq = jnp.sum(row_wide * row_wide, axis=0)
    initial = jnp.zeros((probe_rows, row_feats.shape[1]), jnp.float32)
    piece_feats = lax.all_gather(scaled, "row", axis=1, tiled=True)
    piece_probes = lax.all_gather(probes, "row", axis=1, tiled=True)
    block_cols = block_width(piece_feats.shape[1])

    def advance(position, row_acc):
        column_start = position * block_cols
        feats_block = lax.dynamic_slice_in_dim(piece_feats, column_start, block_cols, 1)
        probes_block = lax.dynamic_slice_in_dim(piece_probes, column_start, block_cols, 1)
        kernel_tile = matern_tile(row_feats, row_sq, feats_block)
        return row_acc + wide_general(probes_block, kernel_tile, ((1,), (1,)))

    folded = lax.fori_loop(0, piece_feats.shape[1] // block_cols, advance, initial)
    column_sums = 0.0
    row_sums = lax.psum_scatter(folded, "col", scatter_dimension=1, tiled=True)
    return row_sums + column_sums


def solution(mesh):
    in_specs = (P(("row", "col"), None), P(), P(), P(), P(), P(None, ("row", "col")))
    out_specs = P(None, ("row", "col"))
    return jax.shard_map(
        on_device, mesh=mesh, in_specs=in_specs, out_specs=out_specs, check_vma=False
    )
```

profile of v0, /device:TPU:8, one launch (start us, length us, event | category | flops | bytes accessed | tf_op | source)
XLA Modules:
  0.0 365.1 jit_solution(8537713413298541568)
XLA Ops:
  6.6 1.3 fusion.9
  8.2 0.5 fusion.10
  9.0 57.5 %all-gather.2 = bf16[16,160,32]{1,2,0:T(8,128)(2,1)S(1)} all-gather(bf16[1,160,32]{1,2,0:T(8,128)(2,1)S(1)} %fusion.12), channel_id=1, replica_groups=mesh['row'=16,'col'=32] {'row'}, dimensions={0}, use_global_device_ids=true | all-gather | bytes 174080 | tf_op jit(solution)/shard_map/all_gather | solution.py:42
  66.5 44.4 %all-gather.1 = bf16[32,160,32]{1,2,0:T(8,128)(2,1)S(1)} all-gather(bf16[1,160,32]{1,2,0:T(8,128)(2,1)S(1)} %fusion.12), channel_id=1, replica_groups=mesh['row'=16,'col'=32] {'col'}, dimensions={0}, use_global_device_ids=true | all-gather | bytes 337920 | tf_op jit(solution)/shard_map/all_gather | solution.py:38
  110.9 45.5 %all-gather = bf16[16,160,8]{1,2,0:T(8,128)(2,1)S(1)} all-gather(bf16[1,160,8]{1,2,0:T(8,128)(2,1)S(1)} %bitcast.48), channel_id=1, replica_groups=mesh['row'=16,'col'=32] {'row'}, dimensions={0}, use_global_device_ids=true | all-gather | bytes 43520 | tf_op jit(solution)/shard_map/all_gather | solution.py:43
  157.3 0.7 reshape.6
  158.2 44.2 %while.14 = (s32[]{:T(128)}, f32[8,5120]{1,0:T(8,128)S(1)}, bf16[8,2560]{1,0:T(8,128)(2,1)S(1)}, f32[5120]{0:T(1024)S(1)}, bf16[32,2560]{1,0:T(8,128)(2,1)S(1)},...) while((s32[]{:T(128)}, f32[8,5120]{1,0:T(8,128)S(1)}, ...), condition=%wide.region_3.4_spmd.clone, body=%wide.region_1.3_spmd.clone.sunk | while | flops 120692488 | bytes 5957809 | solution.py:53
  158.2 3.9 %multiply_convert_fusion.2 = bf16[5120,256]{0,1:T(8,128)(2,1)S(1)} fusion(bf16[32,5120]{1,0:T(8,128)(2,1)S(1)} %get-tuple-element.210, f32[256]{0:T(256)S(1)} %multiply_reduce_fusion.3, f32[5120]{0:T(1024)S(1)} %get-tuple-element.208, bf16[32,2560]{1,0:T(8,128)(2,1)S(1)} %get-tuple-element.209, s32[]{:T(128)S(6)} %select_n.10), kind=kOutput, calls=%fused_computation.7.clone.1 | convolution fusion | flops 99614720 | bytes 2987012 | tf_op jit(solution)/shard_map/while/body/eval_jaxpr/dot_general | solution.py:8
  162.1 0.4 convolution_add_fusion.2
  162.6 3.9 %multiply_convert_fusion.2 = bf16[5120,256]{0,1:T(8,128)(2,1)S(1)} fusion(bf16[32,5120]{1,0:T(8,128)(2,1)S(1)} %get-tuple-element.210, f32[256]{0:T(256)S(1)} %multiply_reduce_fusion.3, f32[5120]{0:T(1024)S(1)} %get-tuple-element.208, bf16[32,2560]{1,0:T(8,128)(2,1)S(1)} %get-tuple-element.209, s32[]{:T(128)S(6)} %select_n.10), kind=kOutput, calls=%fused_computation.7.clone.1 | convolution fusion | flops 99614720 | bytes 2987012 | tf_op jit(solution)/shard_map/while/body/eval_jaxpr/dot_general | solution.py:8
  166.5 0.4 convolution_add_fusion.2
  167.0 3.9 %multiply_convert_fusion.2 = bf16[5120,256]{0,1:T(8,128)(2,1)S(1)} fusion(bf16[32,5120]{1,0:T(8,128)(2,1)S(1)} %get-tuple-element.210, f32[256]{0:T(256)S(1)} %multiply_reduce_fusion.3, f32[5120]{0:T(1024)S(1)} %get-tuple-element.208, bf16[32,2560]{1,0:T(8,128)(2,1)S(1)} %get-tuple-element.209, s32[]{:T(128)S(6)} %select_n.10), kind=kOutput, calls=%fused_computation.7.clone.1 | convolution fusion | flops 99614720 | bytes 2987012 | tf_op jit(solution)/shard_map/while/body/eval_jaxpr/dot_general | solution.py:8
  171.4 3.9 %multiply_convert_fusion.2 = bf16[5120,256]{0,1:T(8,128)(2,1)S(1)} fusion(bf16[32,5120]{1,0:T(8,128)(2,1)S(1)} %get-tuple-element.210, f32[256]{0:T(256)S(1)} %multiply_reduce_fusion.3, f32[5120]{0:T(1024)S(1)} %get-tuple-element.208, bf16[32,2560]{1,0:T(8,128)(2,1)S(1)} %get-tuple-element.209, s32[]{:T(128)S(6)} %select_n.10), kind=kOutput, calls=%fused_computation.7.clone.1 | convolution fusion | flops 99614720 | bytes 2987012 | tf_op jit(solution)/shard_map/while/body/eval_jaxpr/dot_general | solution.py:8
  175.9 3.9 %multiply_convert_fusion.2 = bf16[5120,256]{0,1:T(8,128)(2,1)S(1)} fusion(bf16[32,5120]{1,0:T(8,128)(2,1)S(1)} %get-tuple-element.210, f32[256]{0:T(256)S(1)} %multiply_reduce_fusion.3, f32[5120]{0:T(1024)S(1)} %get-tuple-element.208, bf16[32,2560]{1,0:T(8,128)(2,1)S(1)} %get-tuple-element.209, s32[]{:T(128)S(6)} %select_n.10), kind=kOutput, calls=%fused_computation.7.clone.1 | convolution fusion | flops 99614720 | bytes 2987012 | tf_op jit(solution)/shard_map/while/body/eval_jaxpr/dot_general | solution.py:8
  179.8 0.4 convolution_add_fusion.2
  180.3 3.9 %multiply_convert_fusion.2 = bf16[5120,256]{0,1:T(8,128)(2,1)S(1)} fusion(bf16[32,5120]{1,0:T(8,128)(2,1)S(1)} %get-tuple-element.210, f32[256]{0:T(256)S(1)} %multiply_reduce_fusion.3, f32[5120]{0:T(1024)S(1)} %get-tuple-element.208, bf16[32,2560]{1,0:T(8,128)(2,1)S(1)} %get-tuple-element.209, s32[]{:T(128)S(6)} %select_n.10), kind=kOutput, calls=%fused_computation.7.clone.1 | convolution fusion | flops 99614720 | bytes 2987012 | tf_op jit(solution)/shard_map/while/body/eval_jaxpr/dot_general | solution.py:8
  184.7 3.9 %multiply_convert_fusion.2 = bf16[5120,256]{0,1:T(8,128)(2,1)S(1)} fusion(bf16[32,5120]{1,0:T(8,128)(2,1)S(1)} %get-tuple-element.210, f32[256]{0:T(256)S(1)} %multiply_reduce_fusion.3, f32[5120]{0:T(1024)S(1)} %get-tuple-element.208, bf16[32,2560]{1,0:T(8,128)(2,1)S(1)} %get-tuple-element.209, s32[]{:T(128)S(6)} %select_n.10), kind=kOutput, calls=%fused_computation.7.clone.1 | convolution fusion | flops 99614720 | bytes 2987012 | tf_op jit(solution)/shard_map/while/body/eval_jaxpr/dot_general | solution.py:8
  189.1 3.9 %multiply_convert_fusion.2 = bf16[5120,256]{0,1:T(8,128)(2,1)S(1)} fusion(bf16[32,5120]{1,0:T(8,128)(2,1)S(1)} %get-tuple-element.210, f32[256]{0:T(256)S(1)} %multiply_reduce_fusion.3, f32[5120]{0:T(1024)S(1)} %get-tuple-element.208, bf16[32,2560]{1,0:T(8,128)(2,1)S(1)} %get-tuple-element.209, s32[]{:T(128)S(6)} %select_n.10), kind=kOutput, calls=%fused_computation.7.clone.1 | convolution fusion | flops 99614720 | bytes 2987012 | tf_op jit(solution)/shard_map/while/body/eval_jaxpr/dot_general | solution.py:8
  193.5 3.9 %multiply_convert_fusion.2 = bf16[5120,256]{0,1:T(8,128)(2,1)S(1)} fusion(bf16[32,5120]{1,0:T(8,128)(2,1)S(1)} %get-tuple-element.210, f32[256]{0:T(256)S(1)} %multiply_reduce_fusion.3, f32[5120]{0:T(1024)S(1)} %get-tuple-element.208, bf16[32,2560]{1,0:T(8,128)(2,1)S(1)} %get-tuple-element.209, s32[]{:T(128)S(6)} %select_n.10), kind=kOutput, calls=%fused_computation.7.clone.1 | convolution fusion | flops 99614720 | bytes 2987012 | tf_op jit(solution)/shard_map/while/body/eval_jaxpr/dot_general | solution.py:8
  197.5 0.4 convolution_add_fusion.2
  198.0 3.9 %multiply_convert_fusion.2 = bf16[5120,256]{0,1:T(8,128)(2,1)S(1)} fusion(bf16[32,5120]{1,0:T(8,128)(2,1)S(1)} %get-tuple-element.210, f32[256]{0:T(256)S(1)} %multiply_reduce_fusion.3, f32[5120]{0:T(1024)S(1)} %get-tuple-element.208, bf16[32,2560]{1,0:T(8,128)(2,1)S(1)} %get-tuple-element.209, s32[]{:T(128)S(6)} %select_n.10), kind=kOutput, calls=%fused_computation.7.clone.1 | convolution fusion | flops 99614720 | bytes 2987012 | tf_op jit(solution)/shard_map/while/body/eval_jaxpr/dot_general | solution.py:8
  202.3 2.3 copy.16
  204.6 152.1 %reduce-scatter.4.cloned.1.call-done = f32[160,8]{1,0:T(8,128)} async-done(((f32[5120,8]{1,0:T(8,128)}), f32[160,8]{1,0:T(8,128)}) %reduce-scatter.4.cloned.1.call-update) | async-done | bytes 5136
  356.7 1.6 copy.17
  (34 shorter events, 4.5 us)
Async XLA Ops:
  6.5 1.7 copy-start
  6.5 2.2 copy-start.3
  6.5 2.2 copy-start.2
  6.5 104.3 %copy-start.1 = (bf16[8,160]{1,0:T(8,128)(2,1)S(1)}, bf16[8,160]{1,0:T(8,128)(2,1)}, u32[]{:S(2)}) copy-start(bf16[8,160]{1,0:T(8,128)(2,1)} %param.13) | copy-start | bytes 7684
  6.5 350.2 %reduce-scatter.4.cloned.1.call-start = ((), (), s32[]{:S(2)}) async-start(), calls=%async_computation.1 | async-start | bytes 2703360
Sparse Core Ops, SparseCore 0:
  204.7 151.9 reduce-scatter.3
where the time goes:
time: 365 us
  waiting for transfers between devices  152 us (42%)
  blocking collectives  147 us (40%)
  matrix products  45.8 us (13%)
  between operations  13.5 us (4%)
  local copies, waits for them, and re-layouts  5.77 us (2%)
    unnamed x2, waiting for transfers between devices  152 us
    all_gather x1, blocking collectives, on_device(): piece_feats = lax.all_gather(scaled, 'row', axis=1, tiled=True)  57.5 us
    dot_general x23, matrix products, wide_general(): lax.dot_general(left.astype(jnp.float32), right.astype(jnp.float32), (dim...  45.8 us
    all_gather x1, blocking collectives, on_device(): piece_probes = lax.all_gather(probes, 'row', axis=1, tiled=True)  45.5 us
    all_gather x1, blocking collectives, on_device(): row_feats = lax.all_gather(scaled, 'col', axis=1, tiled=True)  44.4 us
  transfers between devices with their start and end apart: 1, of which 1 were waited for; matrix products, arithmetic and copies ran while one was open for 0% of the time, Pallas kernels for 0%

commit v1 on v0

--- a/solution.py
+++ b/solution.py
@@ -35,7 +35,9 @@
     features = wide_general(w_out, hidden_two, ((0,), (1,)))
     scaled = (features / lengthscale[:, None]).astype(jnp.bfloat16)
     probe_rows = probes.shape[0]
-    row_feats = lax.all_gather(scaled, "col", axis=1, tiled=True)
+    row_feats = jnp.concatenate(
+        lax.all_to_all(jnp.stack([scaled] * lax.axis_size("col")), "col", 0, 0), axis=1
+    )
     row_wide = row_feats.astype(jnp.float32)
     row_sq = jnp.sum(row_wide * row_wide, axis=0)
     initial = jnp.zeros((probe_rows, row_feats.shape[1]), jnp.float32)

time: 365 us -> 334 us (0.915)
  the two profiles are of different devices: /device:TPU:8 before, /device:TPU:24 now
where the time goes in v1:
time: 334 us
  waiting for transfers between devices  154 us (46%)
  blocking collectives  103 us (31%)
  matrix products  45.8 us (14%)
  between operations  13.5 us (4%)
  starting transfers between devices  10.2 us (3%)
  local copies, waits for them, and re-layouts  6.75 us (2%)
    unnamed x2, waiting for transfers between devices  154 us
    all_gather x1, blocking collectives, on_device(): piece_feats = lax.all_gather(scaled, 'row', axis=1, tiled=True)  51.8 us
    all_gather x1, blocking collectives, on_device(): piece_probes = lax.all_gather(probes, 'row', axis=1, tiled=True)  51.3 us
    dot_general x23, matrix products, wide_general(): lax.dot_general(left.astype(jnp.float32), right.astype(jnp.float32), (dim...  45.8 us
    all_to_all x1, starting transfers between devices, on_device(): lax.all_to_all(jnp.stack([scaled] * lax.axis_size('col')), 'col', 0, 0)  10.1 us
  transfers between devices with their start and end apart: 2, of which 1 were waited for; matrix products, arithmetic and copies ran while one was open for 0% of the time, Pallas kernels for 0%

profile of v1, /device:TPU:24, one launch (start us, length us, event | category | flops | bytes accessed | tf_op | source)
XLA Modules:
  0.0 333.9 jit_solution(13572845322661566989)
XLA Ops:
  6.5 1.4 fusion.9
  8.2 0.5 fusion.10
  9.0 0.8 stack.2
  9.8 10.1 %all-to-all-start = ((bf16[32,32,160]{2,1,0:T(8,128)(2,1)}), bf16[32,32,160]{2,1,0:T(8,128)(2,1)S(1)}, u32[]{:S(2)}, u32[]{:S(2)}) async-start(bf16[32,32,160]{2,1,0:T(8,128)(2,1)} %stack.2), calls=%async_computation | async-start | bytes 1048576 | tf_op jit(solution)/shard_map/all_to_all | solution.py:39
  20.0 51.3 %all-gather = bf16[16,160,8]{1,2,0:T(8,128)(2,1)S(1)} all-gather(bf16[1,160,8]{1,2,0:T(8,128)(2,1)S(1)} %bitcast.48), channel_id=1, replica_groups=mesh['row'=16,'col'=32] {'row'}, dimensions={0}, use_global_device_ids=true | all-gather | bytes 43520 | tf_op jit(solution)/shard_map/all_gather | solution.py:45
  71.5 51.8 %all-gather.1 = bf16[16,160,32]{1,2,0:T(8,128)(2,1)S(1)} all-gather(bf16[1,160,32]{1,2,0:T(8,128)(2,1)S(1)} %bitcast.47), channel_id=1, replica_groups=mesh['row'=16,'col'=32] {'row'}, dimensions={0}, use_global_device_ids=true | all-gather | bytes 174080 | tf_op jit(solution)/shard_map/all_gather | solution.py:44
  124.3 0.7 reshape.13
  125.1 44.2 %while.14 = (s32[]{:T(128)}, f32[8,5120]{1,0:T(8,128)S(1)}, bf16[8,2560]{1,0:T(8,128)(2,1)S(1)}, f32[5120]{0:T(1024)S(1)}, bf16[32,2560]{1,0:T(8,128)(2,1)S(1)},...) while((s32[]{:T(128)}, f32[8,5120]{1,0:T(8,128)S(1)}, ...), condition=%wide.region_3.4_spmd.clone, body=%wide.region_1.3_spmd.clone.sunk | while | flops 120692488 | bytes 5957809 | solution.py:55
  125.1 3.9 %multiply_convert_fusion.2 = bf16[5120,256]{0,1:T(8,128)(2,1)S(1)} fusion(bf16[32,5120]{1,0:T(8,128)(2,1)S(1)} %get-tuple-element.210, f32[256]{0:T(256)S(1)} %multiply_reduce_fusion.3, f32[5120]{0:T(1024)S(1)} %get-tuple-element.208, bf16[32,2560]{1,0:T(8,128)(2,1)S(1)} %get-tuple-element.209, s32[]{:T(128)S(6)} %select_n.10), kind=kOutput, calls=%fused_computation.7.clone.1 | convolution fusion | flops 99614720 | bytes 2987012 | tf_op jit(solution)/shard_map/while/body/eval_jaxpr/dot_general | solution.py:8
  129.1 0.4 convolution_add_fusion.2
  129.5 3.9 %multiply_convert_fusion.2 = bf16[5120,256]{0,1:T(8,128)(2,1)S(1)} fusion(bf16[32,5120]{1,0:T(8,128)(2,1)S(1)} %get-tuple-element.210, f32[256]{0:T(256)S(1)} %multiply_reduce_fusion.3, f32[5120]{0:T(1024)S(1)} %get-tuple-element.208, bf16[32,2560]{1,0:T(8,128)(2,1)S(1)} %get-tuple-element.209, s32[]{:T(128)S(6)} %select_n.10), kind=kOutput, calls=%fused_computation.7.clone.1 | convolution fusion | flops 99614720 | bytes 2987012 | tf_op jit(solution)/shard_map/while/body/eval_jaxpr/dot_general | solution.py:8
  134.0 3.9 %multiply_convert_fusion.2 = bf16[5120,256]{0,1:T(8,128)(2,1)S(1)} fusion(bf16[32,5120]{1,0:T(8,128)(2,1)S(1)} %get-tuple-element.210, f32[256]{0:T(256)S(1)} %multiply_reduce_fusion.3, f32[5120]{0:T(1024)S(1)} %get-tuple-element.208, bf16[32,2560]{1,0:T(8,128)(2,1)S(1)} %get-tuple-element.209, s32[]{:T(128)S(6)} %select_n.10), kind=kOutput, calls=%fused_computation.7.clone.1 | convolution fusion | flops 99614720 | bytes 2987012 | tf_op jit(solution)/shard_map/while/body/eval_jaxpr/dot_general | solution.py:8
  138.4 3.9 %multiply_convert_fusion.2 = bf16[5120,256]{0,1:T(8,128)(2,1)S(1)} fusion(bf16[32,5120]{1,0:T(8,128)(2,1)S(1)} %get-tuple-element.210, f32[256]{0:T(256)S(1)} %multiply_reduce_fusion.3, f32[5120]{0:T(1024)S(1)} %get-tuple-element.208, bf16[32,2560]{1,0:T(8,128)(2,1)S(1)} %get-tuple-element.209, s32[]{:T(128)S(6)} %select_n.10), kind=kOutput, calls=%fused_computation.7.clone.1 | convolution fusion | flops 99614720 | bytes 2987012 | tf_op jit(solution)/shard_map/while/body/eval_jaxpr/dot_general | solution.py:8
  142.8 3.9 %multiply_convert_fusion.2 = bf16[5120,256]{0,1:T(8,128)(2,1)S(1)} fusion(bf16[32,5120]{1,0:T(8,128)(2,1)S(1)} %get-tuple-element.210, f32[256]{0:T(256)S(1)} %multiply_reduce_fusion.3, f32[5120]{0:T(1024)S(1)} %get-tuple-element.208, bf16[32,2560]{1,0:T(8,128)(2,1)S(1)} %get-tuple-element.209, s32[]{:T(128)S(6)} %select_n.10), kind=kOutput, calls=%fused_computation.7.clone.1 | convolution fusion | flops 99614720 | bytes 2987012 | tf_op jit(solution)/shard_map/while/body/eval_jaxpr/dot_general | solution.py:8
  146.7 0.4 convolution_add_fusion.2
  147.2 3.9 %multiply_convert_fusion.2 = bf16[5120,256]{0,1:T(8,128)(2,1)S(1)} fusion(bf16[32,5120]{1,0:T(8,128)(2,1)S(1)} %get-tuple-element.210, f32[256]{0:T(256)S(1)} %multiply_reduce_fusion.3, f32[5120]{0:T(1024)S(1)} %get-tuple-element.208, bf16[32,2560]{1,0:T(8,128)(2,1)S(1)} %get-tuple-element.209, s32[]{:T(128)S(6)} %select_n.10), kind=kOutput, calls=%fused_computation.7.clone.1 | convolution fusion | flops 99614720 | bytes 2987012 | tf_op jit(solution)/shard_map/while/body/eval_jaxpr/dot_general | solution.py:8
  151.6 3.9 %multiply_convert_fusion.2 = bf16[5120,256]{0,1:T(8,128)(2,1)S(1)} fusion(bf16[32,5120]{1,0:T(8,128)(2,1)S(1)} %get-tuple-element.210, f32[256]{0:T(256)S(1)} %multiply_reduce_fusion.3, f32[5120]{0:T(1024)S(1)} %get-tuple-element.208, bf16[32,2560]{1,0:T(8,128)(2,1)S(1)} %get-tuple-element.209, s32[]{:T(128)S(6)} %select_n.10), kind=kOutput, calls=%fused_computation.7.clone.1 | convolution fusion | flops 99614720 | bytes 2987012 | tf_op jit(solution)/shard_map/while/body/eval_jaxpr/dot_general | solution.py:8
  156.1 3.9 %multiply_convert_fusion.2 = bf16[5120,256]{0,1:T(8,128)(2,1)S(1)} fusion(bf16[32,5120]{1,0:T(8,128)(2,1)S(1)} %get-tuple-element.210, f32[256]{0:T(256)S(1)} %multiply_reduce_fusion.3, f32[5120]{0:T(1024)S(1)} %get-tuple-element.208, bf16[32,2560]{1,0:T(8,128)(2,1)S(1)} %get-tuple-element.209, s32[]{:T(128)S(6)} %select_n.10), kind=kOutput, calls=%fused_computation.7.clone.1 | convolution fusion | flops 99614720 | bytes 2987012 | tf_op jit(solution)/shard_map/while/body/eval_jaxpr/dot_general | solution.py:8
  160.5 3.9 %multiply_convert_fusion.2 = bf16[5120,256]{0,1:T(8,128)(2,1)S(1)} fusion(bf16[32,5120]{1,0:T(8,128)(2,1)S(1)} %get-tuple-element.210, f32[256]{0:T(256)S(1)} %multiply_reduce_fusion.3, f32[5120]{0:T(1024)S(1)} %get-tuple-element.208, bf16[32,2560]{1,0:T(8,128)(2,1)S(1)} %get-tuple-element.209, s32[]{:T(128)S(6)} %select_n.10), kind=kOutput, calls=%fused_computation.7.clone.1 | convolution fusion | flops 99614720 | bytes 2987012 | tf_op jit(solution)/shard_map/while/body/eval_jaxpr/dot_general | solution.py:8
  164.4 0.4 convolution_add_fusion.2
  164.9 3.9 %multiply_convert_fusion.2 = bf16[5120,256]{0,1:T(8,128)(2,1)S(1)} fusion(bf16[32,5120]{1,0:T(8,128)(2,1)S(1)} %get-tuple-element.210, f32[256]{0:T(256)S(1)} %multiply_reduce_fusion.3, f32[5120]{0:T(1024)S(1)} %get-tuple-element.208, bf16[32,2560]{1,0:T(8,128)(2,1)S(1)} %get-tuple-element.209, s32[]{:T(128)S(6)} %select_n.10), kind=kOutput, calls=%fused_computation.7.clone.1 | convolution fusion | flops 99614720 | bytes 2987012 | tf_op jit(solution)/shard_map/while/body/eval_jaxpr/dot_general | solution.py:8
  169.3 2.3 copy.14
  171.6 153.9 %reduce-scatter.4.cloned.1.call-done = f32[160,8]{1,0:T(8,128)} async-done(((f32[5120,8]{1,0:T(8,128)}), f32[160,8]{1,0:T(8,128)}) %reduce-scatter.4.cloned.1.call-update) | async-done | bytes 5136
  325.5 1.6 copy.15
  (37 shorter events, 5.2 us)
Async XLA Ops:
  6.5 1.7 copy-start
  6.5 2.2 copy-start.3
  6.5 2.2 copy-start.2
  6.5 13.5 %copy-start.1 = (bf16[8,160]{1,0:T(8,128)(2,1)S(1)}, bf16[8,160]{1,0:T(8,128)(2,1)}, u32[]{:S(2)}) copy-start(bf16[8,160]{1,0:T(8,128)(2,1)} %param.13) | copy-start | bytes 7684
  9.8 113.9 %all-to-all-start = ((bf16[32,32,160]{2,1,0:T(8,128)(2,1)}), bf16[32,32,160]{2,1,0:T(8,128)(2,1)S(1)}, u32[]{:S(2)}, u32[]{:S(2)}) async-start(bf16[32,32,160]{2,1,0:T(8,128)(2,1)} %stack.2), calls=%async_computation | async-start | bytes 1048576 | tf_op jit(solution)/shard_map/all_to_all | solution.py:39
  20.0 305.5 %reduce-scatter.4.cloned.1.call-start = ((), (), s32[]{:S(2)}) async-start(), calls=%async_computation.2 | async-start | bytes 2703360
Sparse Core Ops, SparseCore 0:
  171.7 153.7 reduce-scatter.3
